TPU v7x, 32 devices: a whole 2x2x4 slice. The times are simulated.
32 devices in a mesh: dp: 4 (over x, core), label: 8 (over z, y).
Axes of the slice: x: 2, y: 2, z: 4, core: 2. Of those that a mesh axis runs over, the one named last changes fastest.
Arguments:
- token_ids: int32 [64, 2, 32], P(('dp', 'label')), may hold values from 0 to 4095
- labeled: int32 [64], P(('dp', 'label')), may hold values from 0 to 1, as said below
- positive_ids: int32 [64, 16], P(('dp', 'label')), may hold values from 0 to 163839
- vocab_table: bfloat16 [4096, 768], P(('dp', 'label')), may hold values from -6 to 6
- enc_weight: bfloat16 [768, 768], replicated, may hold values from -0.21875 to 0.21875
- label_matrix: bfloat16 [163840, 768], P(('dp', 'label')), may hold values from -0.21875 to 0.21875
- label_log_rates: float32 [163840], P(('dp', 'label')), may hold values from -11.5 to -6.9
Outputs:
- loss: float32 [], replicated
- grad_weight: float32 [768, 768], replicated
- new_log_rates: float32 [163840], P(('dp', 'label'))
Inputs may be any that keep to these rules, and one draw needn't show every extreme that they name: At least one document has labeled = 1.
All inputs are finite; a program needn't handle non-finite values.
Results may differ from a plain program's by a relative error of at most 0.0042.
Values may be sent and summed in bfloat16 or wider, within the bound.
No kernel may reach another device: no remote copies, remote signals or barrier semaphores. Data moves between devices by JAX's collectives and lax.ppermute only.
A program may use at most 128 MiB of HBM per device.

v0:
```python
import jax
import jax.numpy as jnp
from jax import lax
from jax.sharding import PartitionSpec as P


def encode(pooled_rows, enc_weight):
    pre = jnp.dot(pooled_rows, enc_weight, preferred_element_type=jnp.float32)
    inv_norm = lax.rsqrt(jnp.sum(pre * pre, axis=-1, keepdims=True) + 1e-06)
    return (pre * inv_norm, inv_norm)


def tangent(grad_emb, unit_strong, inv_strong):
    return (
        grad_emb - unit_strong * jnp.sum(unit_strong * grad_emb, axis=-1, keepdims=True)
    ) * inv_strong


def outer_sum(pooled_strong, grad_pre):
    return jnp.einsum("dk,dj->kj", pooled_strong, grad_pre, precision=lax.Precision.HIGHEST)


def shards(
    token_ids, labeled, positive_ids, vocab_table, enc_weight, label_matrix, label_log_rates
):
    own_docs = token_ids.shape[0]
    title = token_ids.shape[2]
    width = vocab_table.shape[1]
    vocab_rows = vocab_table.shape[0]
    label_rows = label_matrix.shape[0]
    shard_index = lax.axis_index(("dp", "label"))
    all_tokens, all_labeled, all_positives = (
        lax.all_gather(token_ids, ("dp", "label"), axis=0, tiled=True),
        lax.all_gather(labeled, ("dp", "label"), axis=0, tiled=True),
        lax.all_gather(positive_ids, ("dp", "label"), axis=0, tiled=True),
    )
    docs_all = all_tokens.shape[0]
    flat_tokens = all_tokens.reshape(docs_all * 2, title)
    local_ids = flat_tokens - shard_index * vocab_rows
    vocab_codes = jnp.arange(vocab_rows, dtype=jnp.int32)
    rows = local_ids
    tally = jnp.zeros((lax.axis_size(("dp", "label")) * (own_docs * 2), vocab_rows), jnp.float32)
    for position in range(title):
        tally = tally + (rows[:, position : position + 1] == vocab_codes[None, :]).astype(
            jnp.float32
        )
    pooled_rows = lax.psum_scatter(
        jnp.dot(tally.astype(jnp.bfloat16), vocab_table, preferred_element_type=jnp.float32)
        * (1.0 / title),
        ("dp", "label"),
        scatter_dimension=0,
        tiled=True,
    ).astype(jnp.bfloat16)
    pooled_own = jnp.transpose(pooled_rows.reshape(own_docs, 2, width), (1, 0, 2))
    unit_own, inv_own = encode(pooled_own.reshape(2 * own_docs, width), enc_weight)
    emb_own = unit_own.astype(jnp.bfloat16).reshape(2, own_docs, width)
    scores = (
        jnp.einsum(
            "vrk,lk->vrl",
            lax.all_gather(emb_own, ("dp", "label"), axis=1, tiled=True),
            label_matrix,
            preferred_element_type=jnp.float32,
        )
        * 16.0
        - 6.0
    )
    weak = scores[0]
    strong = scores[1]
    teacher = jax.nn.sigmoid(weak)
    mean_teacher = jnp.mean(teacher, axis=0)
    label_codes = shard_index * label_rows + jnp.arange(label_rows, dtype=jnp.int32)
    hit = jnp.zeros((docs_all, label_rows), dtype=bool)
    for column in range(all_positives.shape[1]):
        hit = hit | (all_positives[:, column : column + 1] == label_codes[None, :])
    flag = (all_labeled == 1)[:, None]
    rates = jnp.exp(label_log_rates)
    target = jnp.where(
        flag, hit.astype(jnp.float32), teacher * rates[None, :] / mean_teacher[None, :]
    )
    total_local = jnp.sum(target)
    loss_local = jnp.sum(jax.nn.softplus(strong) - target * strong)
    slope = (jax.nn.sigmoid(strong) - target).astype(jnp.bfloat16)
    labeled_count = jnp.sum(all_labeled).astype(jnp.float32)
    batch_rate = jnp.sum((flag & hit).astype(jnp.float32), axis=0) / labeled_count
    new_log_rates = jnp.log(0.9 * rates + 0.1 * batch_rate)
    factor = jnp.float32(16.0)
    rows = slope
    grad_emb = lax.psum_scatter(
        jnp.dot(rows, label_matrix, preferred_element_type=jnp.float32) * factor,
        ("dp", "label"),
        scatter_dimension=0,
        tiled=True,
    )
    grad_pre = tangent(grad_emb, unit_own[own_docs:], inv_own[own_docs:])
    weight_local = outer_sum(pooled_own[1].astype(jnp.float32), grad_pre)
    weight_sum, total, loss_sum = lax.psum((weight_local, total_local, loss_local), ("dp", "label"))
    grad_weight = weight_sum / total
    loss = loss_sum / total
    return (loss, grad_weight, new_log_rates)


def solution(mesh):
    return jax.shard_map(
        shards,
        mesh=mesh,
        in_specs=(
            P(("dp", "label"), None, None),
            P(("dp", "label")),
            P(("dp", "label"), None),
            P(("dp", "label"), None),
            P(),
            P(("dp", "label"), None),
            P(("dp", "label")),
        ),
        out_specs=(P(), P(), P(("dp", "label"))),
        check_vma=False,
    )
```

profile of v0, /device:TPU:0, one launch (start us, length us, event | category | flops | bytes accessed | tf_op | source)
XLA Modules:
  0.0 601.3 jit_solution(3730162300531680459)
XLA Ops:
  7.2 0.9 dynamic-update-slice
  8.2 42.0 %all-reduce = s32[64]{0:T(128)S(1)} all-reduce(s32[64]{0:T(128)S(1)} %dynamic-update-slice), channel_id=1, replica_groups=mesh['dp'=4,'label'=8] {'dp','label'}, use_global_device_ids=true, to_apply=%add | all-reduce | flops 64 | bytes 512
  51.3 66.4 %all_gather.12 = s32[64,2,32]{2,1,0:T(2,128)S(1)} all-gather(s32[2,2,32]{2,1,0:T(2,128)} %param.7), channel_id=1, replica_groups=mesh['dp'=4,'label'=8] {'dp','label'}, dimensions={0}, use_global_device_ids=true | all-gather | bytes 16896 | tf_op jit(solution)/shard_map/all_gather | solution.py:33
  119.1 63.5 %all-gather = s32[32,2,16]{2,1,0:T(2,128)S(1)} all-gather(s32[1,2,16]{2,1,0:T(2,128)S(1)} %bitcast.122), channel_id=1, replica_groups=mesh['dp'=4,'label'=8] {'dp','label'}, dimensions={0}, use_global_device_ids=true | all-gather | bytes 4224 | tf_op jit(solution)/shard_map/all_gather | solution.py:35
  182.6 0.8 fusion.65
  184.2 0.8 copy.204
  185.1 0.8 copy.203
  185.9 0.8 copy.202
  186.8 0.8 copy.201
  187.6 0.8 copy.200
  189.3 1.4 copy.198
  190.6 1.3 copy.197
  196.5 43.1 %all-reduce.11 = bf16[128,768]{1,0:T(8,128)(2,1)S(1)} all-reduce(f32[128,768]{1,0:T(8,128)S(1)} %convolution_multiply_fusion), channel_id=2, replica_groups=mesh['dp'=4,'label'=8] {'dp','label'}, use_global_device_ids=true, to_apply=%region_0.0.clone | all-reduce | flops 98304 | bytes 589824
  240.2 65.1 %all_gather.13 = bf16[2,64,768]{2,0,1:T(2,128)(2,1)S(1)} all-gather(bf16[2,2,768]{2,0,1:T(2,128)(2,1)S(1)} %copy.140), channel_id=1, replica_groups=mesh['dp'=4,'label'=8] {'dp','label'}, dimensions={1}, use_global_device_ids=true | all-gather | bytes 202752 | tf_op jit(solution)/shard_map/all_gather | solution.py:60
  305.3 5.9 fusion.5
  311.9 2.7 convert_reduce_fusion
  315.3 3.4 fusion.60
  318.6 5.5 convolution_multiply_fusion.1
  324.2 122.2 %all-reduce.10.cloned.1.call-done = f32[64,768]{1,0:T(8,128)} async-done(((f32[64,768]{1,0:T(8,128)}), f32[64,768]{1,0:T(8,128)}) %all-reduce.10.cloned.1.call-update) | async-done | bytes 196624
  446.4 0.9 multiply_reduce_fusion.1
  447.3 3.3 fusion.50
  450.6 41.7 %all-reduce.3 = (f32[]{:T(128)}, f32[]{:T(128)}) all-reduce(f32[]{:T(128)} %get-tuple-element.4, f32[]{:T(128)} %get-tuple-element.3), channel_id=1, replica_groups=mesh['dp'=4,'label'=8] {'dp','label'}, use_global_device_ids=true, to_apply=%region_4.5 | all-reduce | flops 2 | bytes 16 | tf_op jit(solution)/shard_map/psum | solution.py:96
  493.6 95.9 %all-reduce.8.cloned.1.call-done = f32[768,768]{1,0:T(8,128)} async-done(((f32[768,768]{1,0:T(8,128)}), f32[768,768]{1,0:T(8,128)}) %all-reduce.8.cloned.1.call-update) | async-done | bytes 2359312 | tf_op jit(solution)/shard_map/psum | solution.py:96
  589.5 3.9 broadcast_divide_fusion
  (82 shorter events, 10.0 us)
Async XLA Ops:
  7.2 232.5 %copy-start = (bf16[768,768]{1,0:T(8,128)(2,1)S(1)}, bf16[768,768]{1,0:T(8,128)(2,1)}, u32[]{:S(2)}) copy-start(bf16[768,768]{1,0:T(8,128)(2,1)} %param.11) | copy-start | bytes 3538948
  7.2 439.2 %all-reduce.10.cloned.1.call-start = ((), (), s32[]{:S(2)}) async-start(), calls=%async_computation.1 | async-start | bytes 393216
  118.0 1.1 copy-start.6
  193.0 2.6 copy-start.7
  311.2 0.7 copy-start.2
  311.2 0.7 copy-start.3
  311.2 0.7 copy-start.4
  311.2 0.7 copy-start.5
  311.2 3.4 copy-start.1
  324.1 265.4 %all-reduce.8.cloned.1.call-start = ((), (), s32[]{:S(2)}) async-start(), calls=%async_computation | async-start | bytes 4718592 | tf_op jit(solution)/shard_map/psum | solution.py:96
Sparse Core Ops, SparseCore 0:
  324.2 122.1 all-reduce.9
  452.5 136.9 all-reduce.7
where the time goes:
time: 603 us; the launch traced here: 601 us
  blocking collectives  322 us (53%)
  waiting for transfers between devices  218 us (36%)
  between operations  17.4 us (3%)
  matrix products  15.8 us (3%)
  local copies, waits for them, and re-layouts  15.1 us (3%)
  other arithmetic  13 us (2%)
    unnamed x3, waiting for transfers between devices  122 us
    psum x1, waiting for transfers between devices, shards(): lax.psum((weight_local, total_local, loss_local), ('dp', 'label'))  95.9 us
    unnamed x2, blocking collectives  85 us
    all_gather x1, blocking collectives, shards(): lax.all_gather(token_ids, ('dp', 'label'), axis=0, tiled=True)  66.4 us
    all_gather x1, blocking collectives, shards(): lax.all_gather(emb_own, ('dp', 'label'), axis=1, tiled=True)  65.1 us
    all_gather x1, blocking collectives, shards(): lax.all_gather(positive_ids, ('dp', 'label'), axis=0, tiled=True)  63.5 us
    psum x1, blocking collectives, shards(): lax.psum((weight_local, total_local, loss_local), ('dp', 'label'))  41.7 us
    unnamed x66, local copies, waits for them, and re-layouts  13.5 us
  transfers between devices with their start and end apart: 2, of which 2 were waited for; matrix products, arithmetic and copies ran while one was open for 0% of the time, Pallas kernels for 0%

commit v1 on v0

--- a/solution.py
+++ b/solution.py
@@ -2,6 +2,28 @@
 import jax.numpy as jnp
 from jax import lax
 from jax.sharding import PartitionSpec as P
+
+
+def joined_along(blocks, dim):
+    blocks = jnp.moveaxis(blocks, 0, dim)
+    shape = blocks.shape
+    return blocks.reshape(*shape[:dim], shape[dim] * shape[dim + 1], *shape[dim + 2 :])
+
+
+def grow_blocks(value, axis):
+    size = lax.axis_size(axis)
+    blocks = value[None]
+    for level in range(size.bit_length() - 1):
+        bit = 1 << level
+        theirs = lax.ppermute(blocks, axis, [(i, i ^ bit) for i in range(size)])
+        both = jnp.stack([blocks, theirs])
+        upper = lax.axis_index(axis) >> level & 1
+        blocks = jnp.where(upper == 0, both, both[::-1]).reshape(-1, *value.shape)
+    return blocks
+
+
+def gather_by_bits(x, axis, dim):
+    return joined_along(grow_blocks(x, axis), dim)
 
 
 def encode(pooled_rows, enc_weight):
@@ -57,7 +79,7 @@
     scores = (
         jnp.einsum(
             "vrk,lk->vrl",
-            lax.all_gather(emb_own, ("dp", "label"), axis=1, tiled=True),
+            gather_by_bits(emb_own, ("dp", "label"), 1),
             label_matrix,
             preferred_element_type=jnp.float32,
         )

time: 603 us -> 543 us (0.900)
  blocking collectives: 322 us -> 255 us
  local copies, waits for them, and re-layouts: 15.1 us -> 5.13 us
  starting transfers between devices: 0.08 us -> 8.98 us
  waiting for transfers between devices: 218 us -> 226 us
    all_gather x1 -> x0, blocking collectives: 65.1 us -> none  [shards(): lax.all_gather(emb_own, ('dp', 'label'), axis=1, tiled=True)]
    unnamed x66 -> x60, local copies, waits for them, and re-layouts: 13.5 us -> 3.98 us
    ppermute x0 -> x5, starting transfers between devices: none -> 8.9 us  [grow_blocks(): theirs = lax.ppermute(blocks, axis, [(i, i ^ bit) for i in range(size)])]
    unnamed x2, blocking collectives: 85 us -> 78.9 us
  transfers between devices with their start and end apart: 2 -> 7, of which waited for: 2 -> 5; matrix products, arithmetic and copies ran while one was open for 0% -> 1% of each run, Pallas kernels for 0% -> 0%
where the time goes in v1:
time: 543 us; the launch traced here: 542 us
  blocking collectives  255 us (47%)
  waiting for transfers between devices  226 us (42%)
  between operations  17.6 us (3%)
  matrix products  15.8 us (3%)
  other arithmetic  13.4 us (2%)
  starting transfers between devices  8.98 us (2%)
    unnamed x3, waiting for transfers between devices  125 us
    psum x1, waiting for transfers between devices, shards(): lax.psum((weight_local, total_local, loss_local), ('dp', 'label'))  95.8 us
    unnamed x2, blocking collectives  78.9 us
    all_gather x1, blocking collectives, shards(): lax.all_gather(token_ids, ('dp', 'label'), axis=0, tiled=True)  70.4 us
    all_gather x1, blocking collectives, shards(): lax.all_gather(positive_ids, ('dp', 'label'), axis=0, tiled=True)  64.1 us
    psum x1, blocking collectives, shards(): lax.psum((weight_local, total_local, loss_local), ('dp', 'label'))  41.7 us
  transfers between devices with their start and end apart: 7, of which 5 were waited for; matrix products, arithmetic and copies ran while one was open for 1% of the time, Pallas kernels for 0%

profile of v1, /device:TPU:0, one launch (start us, length us, event | category | flops | bytes accessed | tf_op | source)
XLA Modules:
  0.0 542.2 jit_solution(17520291304486819196)
XLA Ops:
  7.2 70.4 %all_gather.9 = s32[64,2,32]{2,1,0:T(2,128)S(1)} all-gather(s32[2,2,32]{2,1,0:T(2,128)} %param.7), channel_id=1, replica_groups=mesh['dp'=4,'label'=8] {'dp','label'}, dimensions={0}, use_global_device_ids=true | all-gather | bytes 16896 | tf_op jit(solution)/shard_map/all_gather | solution.py:55
  80.9 0.8 convolution_multiply_fusion
  81.7 41.6 %all-reduce.11 = bf16[128,768]{1,0:T(8,128)(2,1)S(1)} all-reduce(f32[128,768]{1,0:T(8,128)S(1)} %convolution_multiply_fusion), channel_id=2, replica_groups=mesh['dp'=4,'label'=8] {'dp','label'}, use_global_device_ids=true, to_apply=%region_0.0.clone | all-reduce | flops 98304 | bytes 589824
  123.9 1.4 collective-permute-start
  125.3 64.1 %all-gather = s32[32,2,16]{2,1,0:T(2,128)S(1)} all-gather(s32[1,2,16]{2,1,0:T(2,128)S(1)} %bitcast.153), channel_id=1, replica_groups=mesh['dp'=4,'label'=8] {'dp','label'}, dimensions={0}, use_global_device_ids=true | all-gather | bytes 4224 | tf_op jit(solution)/shard_map/all_gather | solution.py:57
  189.9 37.4 %all-reduce = s32[64]{0:T(128)S(1)} all-reduce(s32[64]{0:T(128)S(1)} %dynamic-update-slice), channel_id=1, replica_groups=mesh['dp'=4,'label'=8] {'dp','label'}, use_global_device_ids=true, to_apply=%add | all-reduce | flops 64 | bytes 512
  227.3 2.9 collective-permute-start.1
  230.2 1.7 collective-permute-done.1
  232.0 2.2 collective-permute-start.2
  235.4 1.4 collective-permute-done.2
  237.0 2.7 convert_reduce_fusion
  239.7 0.6 reduce_sum.69
  241.3 2.3 collective-permute-start.4
  243.7 0.6 add_log_fusion
  244.3 2.8 collective-permute-done.4
  247.6 5.9 %fusion.5 = f32[2,64,5120]{2,1,0:T(8,128)S(1)} fusion(bf16[2,64,768]{2,1,0:T(8,128)(2,1)S(1)} %reshape.73, bf16[5120,768]{1,0:T(8,128)(2,1)} %param.12), kind=kOutput, calls=%fused_computation.3 | convolution fusion | flops 1007943680 | bytes 10682368 | tf_op jit(solution)/shard_map/vrk,lk->vrl/dot_general | solution.py:80
  253.9 3.4 fusion.61
  257.3 5.5 %convolution_multiply_fusion.1 = f32[64,768]{1,0:T(8,128)} fusion(bf16[5120,768]{1,0:T(8,128)(2,1)} %param.12, f32[64,5120]{1,0:T(8,128)S(1)} %get-tuple-element.7, f32[2,64,5120]{2,1,0:T(8,128)S(1)} %fusion.5), kind=kOutput, calls=%fused_computation.20 | convolution fusion | flops 505004032 | bytes 10682368 | tf_op jit(solution)/shard_map/dot_general | solution.py:111
  262.9 124.5 %all-reduce.10.cloned.1.call-done = f32[64,768]{1,0:T(8,128)} async-done(((f32[64,768]{1,0:T(8,128)}), f32[64,768]{1,0:T(8,128)}) %all-reduce.10.cloned.1.call-update) | async-done | bytes 196624
  387.4 0.9 multiply_reduce_fusion.1
  388.2 3.3 fusion.49
  391.5 41.7 %all-reduce.3 = (f32[]{:T(128)}, f32[]{:T(128)}) all-reduce(f32[]{:T(128)} %get-tuple-element.4, f32[]{:T(128)} %get-tuple-element.3), channel_id=1, replica_groups=mesh['dp'=4,'label'=8] {'dp','label'}, use_global_device_ids=true, to_apply=%region_4.5 | all-reduce | flops 2 | bytes 16 | tf_op jit(solution)/shard_map/psum | solution.py:118
  434.5 95.8 %all-reduce.8.cloned.1.call-done = f32[768,768]{1,0:T(8,128)} async-done(((f32[768,768]{1,0:T(8,128)}), f32[768,768]{1,0:T(8,128)}) %all-reduce.8.cloned.1.call-update) | async-done | bytes 2359312 | tf_op jit(solution)/shard_map/psum | solution.py:118
  530.4 3.9 broadcast_divide_fusion
  (97 shorter events, 7.1 us)
Async XLA Ops:
  7.2 116.2 %copy-start = (bf16[768,768]{1,0:T(8,128)(2,1)S(1)}, bf16[768,768]{1,0:T(8,128)(2,1)}, u32[]{:S(2)}) copy-start(bf16[768,768]{1,0:T(8,128)(2,1)} %param.11) | copy-start | bytes 3538948
  7.2 380.2 %all-reduce.10.cloned.1.call-start = ((), (), s32[]{:S(2)}) async-start(), calls=%async_computation.1 | async-start | bytes 393216
  78.3 2.6 copy-start.3
  81.7 43.6 %copy-start.2 = (s32[2,16]{1,0:T(2,128)S(1)}, s32[2,16]{1,0:T(2,128)}, u32[]{:S(2)}) copy-start(s32[2,16]{1,0:T(2,128)} %param.9) | copy-start | bytes 388
  123.3 66.4 %copy-start.4 = (s32[2]{0:T(128)S(1)}, s32[2]{0:T(128)}, u32[]{:S(2)}) copy-start(s32[2]{0:T(128)} %param.8) | copy-start | bytes 28
  123.9 103.4 %collective-permute-start = (bf16[1,2,2,768]{3,2,1,0:T(2,128)(2,1)S(1)}, bf16[1,2,2,768]{3,2,1,0:T(2,128)(2,1)S(1)}, u32[]{:S(2)}, u32[]{:S(2)}) collective-permute-start(bf16[1,2,2,768]{3,2,1,0:T(2,128)(2,1)S(1)} %broadcast_in_dim_reshape.3), channel_id=1, source_target_pairs={{0,1},{1,0},{2,3},{3,2},{4,5},{5,4},{6,7},{7,6},{8,9},{9,8},{10,11... | collective-permute-start | bytes 18440 | tf_op jit(solution)/shard_map/ppermute | solution.py:18
  189.4 54.3 %copy-start.1 = (f32[5120]{0:T(1024)S(1)}, f32[5120]{0:T(1024)}, u32[]{:S(2)}) copy-start(f32[5120]{0:T(1024)} %param.13) | copy-start | bytes 61444
  227.3 4.6 collective-permute-start.1
  232.0 4.8 collective-permute-start.2
  236.9 4.1 collective-permute-start.3
  241.3 5.8 %collective-permute-start.4 = (bf16[16,2,2,768]{3,2,0,1:T(2,128)(2,1)S(1)}, bf16[16,2,2,768]{3,2,0,1:T(2,128)(2,1)S(1)}, u32[]{:S(2)}, u32[]{:S(2)}) collective-permute-start(bf16[16,2,2,768]{3,2,0,1:T(2,128)(2,1)S(1)} %bitcast.107), channel_id=1, source_target_pairs={{0,16},{1,17},{2,18},{3,19},{4,20},{5,21},{6,22},{7,23},{8,24},{9,... | collective-permute-start | bytes 294920 | tf_op jit(solution)/shard_map/ppermute | solution.py:18
  262.8 267.6 %all-reduce.8.cloned.1.call-start = ((), (), s32[]{:S(2)}) async-start(), calls=%async_computation | async-start | bytes 4718592 | tf_op jit(solution)/shard_map/psum | solution.py:118
Sparse Core Ops, SparseCore 0:
  262.9 124.4 all-reduce.9
  393.5 136.8 all-reduce.7
